TPU v7x, 32 devices: a whole 2x2x4 slice. The times are simulated.
32 devices in a mesh: leaf: 8 (over z, y), panel: 4 (over x, core).
Axes of the slice: x: 2, y: 2, z: 4, core: 2. Of those that a mesh axis runs over, the one named last changes fastest.
Arguments:
- interface_block: float32 [8, 2048, 2048], P('leaf', 'panel'), may hold values from -0.125 to 0.125
- coupling: bfloat16 [8, 2048, 128], P('leaf', 'panel'), may hold values from -0.375 to 0.375
- eigenvalues: float32 [8, 128], P('leaf'), may hold values from 0.5 to 8
- mode_counts: int32 [8], P('leaf'), may hold values from 64 to 128, as said below
- interface_coords: bfloat16 [8, 2048, 1024], P('leaf', 'panel'), may hold values from -6 to 6
- modal_coords: bfloat16 [8, 128, 4096], P('leaf'), may hold values from -6 to 6
Outputs:
- mode_shapes: float32 [8, 2048, 1024], P('leaf', 'panel')
Inputs may be any that keep to these rules, and one draw needn't show every extreme that they name: `mode_counts`: modes kept by each substructure; some substructure keeps all 128.
All inputs are finite; a program needn't handle non-finite values.
Results may differ from a plain program's by a relative error of at most 0.0023.
Values may be sent and summed in bfloat16 or wider, within the bound.
No kernel may reach another device: no remote copies, remote signals or barrier semaphores. Data moves between devices by JAX's collectives and lax.ppermute only.
A program may use at most 128 MiB of HBM per device.

v0:
```python
import jax
import jax.numpy as jnp
from jax import lax
from jax.sharding import PartitionSpec as P

LEVELS = 2


def partner(value, axis, bit):
    return lax.ppermute(value, axis, [(i, i ^ 1 << bit) for i in range(lax.axis_size(axis))])


def modal_reduce(summed, levels):
    leaf_index = lax.axis_index("leaf")
    current = summed
    for level in range(levels - 1, -1, -1):
        half = current.shape[1] // 2
        my_bit = leaf_index >> level & 1
        keep = lax.dynamic_slice_in_dim(current, my_bit * half, half, 1)
        other = lax.dynamic_slice_in_dim(current, (1 - my_bit) * half, half, 1)
        current = keep + partner(other, "leaf", level)
    return current


def on_device(interface_block, coupling, eigenvalues, mode_counts, interface_coords, modal_coords):
    block = interface_block[0]
    coup = coupling[0]
    coords = interface_coords[0]
    modal = modal_coords[0]
    width = coup.shape[1]
    levels = LEVELS
    index = jnp.arange(width, dtype=jnp.int32)
    mask = (index < mode_counts[0]).astype(jnp.float32)
    scaled = (coup.astype(jnp.float32) * (mask / eigenvalues[0])[None, :]).astype(jnp.bfloat16)
    columns = block
    schur = columns - lax.dot_general(
        scaled,
        lax.all_gather(coup, "panel", axis=0, tiled=True),
        (((1,), (1,)), ((), ())),
        preferred_element_type=jnp.float32,
    )
    merged = schur
    for level in range(levels):
        merged = merged + partner(merged, "leaf", level)
    owned = modal_reduce(jnp.dot(scaled, modal, preferred_element_type=jnp.float32), levels)
    columns = merged
    shapes = owned + jnp.dot(
        columns,
        lax.all_gather(coords, "panel", axis=0, tiled=True).astype(jnp.float32),
        precision=lax.Precision.HIGHEST,
    )
    return shapes[None]


def solution(mesh):
    placed = (
        P("leaf", "panel", None),
        P("leaf", "panel", None),
        P("leaf", None),
        P("leaf"),
        P("leaf", "panel", None),
        P("leaf", None, None),
    )
    return jax.shard_map(
        on_device, mesh=mesh, in_specs=placed, out_specs=P("leaf", "panel", None), check_vma=False
    )
```

profile of v0, /device:TPU:0, one launch (start us, length us, event | category | flops | bytes accessed | tf_op | source)
XLA Modules:
  0.0 233.8 jit_solution(16396193473058666457)
XLA Ops:
  6.5 0.0 copy-start
  6.5 0.0 all-gather.4.cloned.1.call-start
  7.3 8.9 %all-gather = bf16[1,2048,128]{2,1,0:T(8,128)(2,1)S(1)} all-gather(bf16[1,512,128]{2,1,0:T(8,128)(2,1)} %param.7), channel_id=2, replica_groups=mesh['leaf'=8,'panel'=4] {'panel'}, dimensions={1}, use_global_device_ids=true | all-gather | bytes 655360 | tf_op jit(solution)/shard_map/all_gather | solution.py:38
  16.1 0.7 fusion.15
  16.8 5.0 %bitcast_subtract_fusion = f32[512,2048]{1,0:T(8,128)} fusion(f32[1,512,2048]{2,1,0:T(8,128)} %param.6, bf16[1,2048,128]{2,1,0:T(8,128)(2,1)S(1)} %all-gather, bf16[1,512,128]{2,1,0:T(8,128)(2,1)} %param.7, f32[128]{0:T(128)S(1)} %fusion.15), kind=kOutput, calls=%fused_computation.2 | convolution fusion | flops 269680640 | bytes 9044480 | tf_op jit(solution)/shard_map/dot_general | solution.py:36
  21.8 1.5 collective-permute-start.2
  23.3 0.0 copy-done.3
  23.3 1.2 fusion.3
  24.6 2.4 %constant_dynamic-slice_fusion.1 = f32[512,2048]{1,0:T(8,128)} fusion(f32[512,4096]{1,0:T(8,128)S(1)} %fusion.3, s32[]{:T(128)S(6)} %select_n.13), kind=kLoop, calls=%fused_computation.19 | loop fusion | bytes 8388612 | tf_op jit(solution)/shard_map/dynamic_slice | solution.py:20
  27.0 2.1 copy-done.1
  29.1 1.6 collective-permute-start
  30.7 0.0 all-gather.4.cloned.1.call-update
  30.7 84.2 %collective-permute-done.2 = f32[512,2048]{1,0:T(8,128)} collective-permute-done((f32[512,2048]{1,0:T(8,128)}, f32[512,2048]{1,0:T(8,128)}, u32[]{:S(2)}, u32[]{:S(2)}) %collective-permute-start.2) | collective-permute-done | bytes 4194336 | tf_op jit(solution)/shard_map/ppermute | solution.py:10
  114.9 6.5 %add.33 = f32[512,2048]{1,0:T(8,128)} add(f32[512,2048]{1,0:T(8,128)} %bitcast_subtract_fusion, f32[512,2048]{1,0:T(8,128)} %collective-permute-done.2) | non-fusion elementwise | flops 1048576 | bytes 12582912 | tf_op jit(solution)/shard_map/add | solution.py:44
  121.4 1.6 collective-permute-start.3
  123.0 0.0 collective-permute-done
  123.0 4.2 %dynamic-slice_add_fusion = f32[512,2048]{1,0:T(8,128)S(1)} fusion(f32[512,2048]{1,0:T(8,128)} %collective-permute-done, f32[512,4096]{1,0:T(8,128)} %copy-done.1, s32[]{:T(128)S(6)} %select_n.12), kind=kLoop, calls=%fused_computation.4 | loop fusion | flops 1048576 | bytes 12582916 | tf_op jit(solution)/shard_map/add | solution.py:21
  127.3 0.0 copy-start.2
  127.3 1.9 copy-done.2
  129.2 0.1 constant_dynamic-slice_fusion
  129.3 1.6 collective-permute-start.1
  130.9 45.3 %collective-permute-done.1 = f32[512,1024]{1,0:T(8,128)} collective-permute-done((f32[512,1024]{1,0:T(8,128)S(1)}, f32[512,1024]{1,0:T(8,128)}, u32[]{:S(2)}, u32[]{:S(2)}) %collective-permute-start.1) | collective-permute-done | bytes 2097184 | tf_op jit(solution)/shard_map/ppermute | solution.py:10
  176.2 37.5 %collective-permute-done.3 = f32[512,2048]{1,0:T(8,128)} collective-permute-done((f32[512,2048]{1,0:T(8,128)}, f32[512,2048]{1,0:T(8,128)}, u32[]{:S(2)}, u32[]{:S(2)}) %collective-permute-start.3) | collective-permute-done | bytes 4194336 | tf_op jit(solution)/shard_map/ppermute | solution.py:10
  213.7 13.3 %add_bitcast_fusion = f32[1,512,1024]{2,1,0:T(8,128)} fusion(f32[512,1024]{1,0:T(8,128)} %collective-permute-done.1, f32[512,2048]{1,0:T(8,128)} %copy-done.2, s32[]{:T(128)S(6)} %select_n.14, bf16[1,2048,1024]{2,1,0:T(8,128)(2,1)} %all-gather.4.cloned.1.call-done, f32[512,2048]{1,0:T(8,128)} %add.33, f32[512,2048]{1,0:T(8,128)} %collective-permute-done.3), kind=kOutput, calls=%fused_computation.5 | convolution fusion | flops 12886999040 | bytes 18874372 | tf_op jit(solution)/shard_map/dot_general | solution.py:47
  (4 shorter events, 0.0 us)
Async XLA Ops:
  6.5 16.8 %copy-start = (bf16[1,128,4096]{2,1,0:T(8,128)(2,1)S(1)}, bf16[1,128,4096]{2,1,0:T(8,128)(2,1)}, u32[]{:S(2)}) copy-start(bf16[1,128,4096]{2,1,0:T(8,128)(2,1)} %param.11) | copy-start | bytes 3145732
  6.5 169.7 %all-gather.4.cloned.1.call-start = ((), (), s32[]{:S(2)}) async-start(), calls=%async_computation | async-start | bytes 5242880 | tf_op jit(solution)/shard_map/all_gather | solution.py:49
  16.8 6.5 %copy-start.3 = (bf16[1,512,128]{2,1,0:T(8,128)(2,1)S(1)}, bf16[1,512,128]{2,1,0:T(8,128)(2,1)}, u32[]{:S(2)}) copy-start(bf16[1,512,128]{2,1,0:T(8,128)(2,1)} %param.7) | copy-start | bytes 393220
  21.8 93.1 %collective-permute-start.2 = (f32[512,2048]{1,0:T(8,128)}, f32[512,2048]{1,0:T(8,128)}, u32[]{:S(2)}, u32[]{:S(2)}) collective-permute-start(f32[512,2048]{1,0:T(8,128)} %bitcast_subtract_fusion), channel_id=1, source_target_pairs={{0,4},{4,0},{8,12},{12,8},{16,20},{20,16},{24,28},{28,24},{1,5},{5... | collective-permute-start | bytes 12582920 | tf_op jit(solution)/shard_map/ppermute | solution.py:10
  24.6 4.5 %copy-start.1 = (f32[512,4096]{1,0:T(8,128)}, f32[512,4096]{1,0:T(8,128)S(1)}, u32[]{:S(2)}) copy-start(f32[512,4096]{1,0:T(8,128)S(1)} %fusion.3) | copy-start | bytes 25165828
  29.1 93.9 %collective-permute-start = (f32[512,2048]{1,0:T(8,128)}, f32[512,2048]{1,0:T(8,128)}, u32[]{:S(2)}, u32[]{:S(2)}) collective-permute-start(f32[512,2048]{1,0:T(8,128)} %constant_dynamic-slice_fusion.1), channel_id=1, source_target_pairs={{0,8},{4,12},{8,0},{12,4},{16,24},{20,28},{24,16},{28,20},{1,9},{5... | collective-permute-start | bytes 12582920 | tf_op jit(solution)/shard_map/ppermute | solution.py:10
  121.4 92.3 %collective-permute-start.3 = (f32[512,2048]{1,0:T(8,128)}, f32[512,2048]{1,0:T(8,128)}, u32[]{:S(2)}, u32[]{:S(2)}) collective-permute-start(f32[512,2048]{1,0:T(8,128)} %add.33), channel_id=1, source_target_pairs={{0,8},{4,12},{8,0},{12,4},{16,24},{20,28},{24,16},{28,20},{1,9},{5... | collective-permute-start | bytes 12582920 | tf_op jit(solution)/shard_map/ppermute | solution.py:10
  127.3 1.9 copy-start.2
  129.3 46.9 %collective-permute-start.1 = (f32[512,1024]{1,0:T(8,128)S(1)}, f32[512,1024]{1,0:T(8,128)}, u32[]{:S(2)}, u32[]{:S(2)}) collective-permute-start(f32[512,1024]{1,0:T(8,128)S(1)} %constant_dynamic-slice_fusion), channel_id=1, source_target_pairs={{0,4},{4,0},{8,12},{12,8},{16,20},{20,16},{24,28},{28,24},{1,5},{5... | collective-permute-start | bytes 6291464 | tf_op jit(solution)/shard_map/ppermute | solution.py:10
Sparse Core Ops, SparseCore 0:
  30.8 33.3 all-gather.3
where the time goes:
time: 234 us
  waiting for transfers between devices  167 us (71%)
  matrix products  19.5 us (8%)
  between operations  14.2 us (6%)
  other arithmetic  11.4 us (5%)
  blocking collectives  8.86 us (4%)
  local copies, waits for them, and re-layouts  6.59 us (3%)
  starting transfers between devices  6.26 us (3%)
    ppermute x4, waiting for transfers between devices, partner(): lax.ppermute(value, axis, [(i, i ^ 1 << bit) for i in range(lax.axis_size...  167 us
    dot_general x1, matrix products, on_device(): jnp.dot(columns, lax.all_gather(coords, 'panel', axis=0, tiled=True).asty...  13.3 us
    all_gather x1, blocking collectives, on_device(): lax.all_gather(coup, 'panel', axis=0, tiled=True)  8.86 us
    add x1, other arithmetic, on_device(): merged = merged + partner(merged, 'leaf', level)  6.52 us
    ppermute x4, starting transfers between devices, partner(): lax.ppermute(value, axis, [(i, i ^ 1 << bit) for i in range(lax.axis_size...  6.26 us
    dot_general x1, matrix products, on_device(): lax.dot_general(scaled, lax.all_gather(coup, 'panel', axis=0, tiled=True)...  4.98 us
  transfers between devices with their start and end apart: 5, of which 3 were waited for; matrix products, arithmetic and copies ran while one was open for 6% of the time, Pallas kernels for 0%

commit v1 on v0

--- a/solution.py
+++ b/solution.py
@@ -4,6 +4,11 @@
 from jax.sharding import PartitionSpec as P
 
 LEVELS = 2
+
+
+def tiled_gather(x, axis, dim):
+    copies = jnp.concatenate([x] * lax.axis_size(axis), axis=dim)
+    return lax.all_to_all(copies, axis, dim, dim, tiled=True)
 
 
 def partner(value, axis, bit):
@@ -35,7 +40,7 @@
     columns = block
     schur = columns - lax.dot_general(
         scaled,
-        lax.all_gather(coup, "panel", axis=0, tiled=True),
+        tiled_gather(coup, "panel", 0),
         (((1,), (1,)), ((), ())),
         preferred_element_type=jnp.float32,
     )

time: 234 us -> 238 us (1.017)
  blocking collectives: 8.86 us -> 0 us
  waiting for transfers between devices: 167 us -> 173 us
  starting transfers between devices: 6.26 us -> 11.4 us
    all_gather x1 -> x0, blocking collectives: 8.86 us -> none  [on_device(): lax.all_gather(coup, 'panel', axis=0, tiled=True)]
    all_to_all x0 -> x1, waiting for transfers between devices: none -> 7.5 us  [tiled_gather(): return lax.all_to_all(copies, axis, dim, dim, tiled=True)]
    all_to_all x0 -> x1, starting transfers between devices: none -> 4.24 us  [tiled_gather(): return lax.all_to_all(copies, axis, dim, dim, tiled=True)]
  transfers between devices with their start and end apart: 5 -> 6, of which waited for: 3 -> 4; matrix products, arithmetic and copies ran while one was open for 6% -> 6% of each run, Pallas kernels for 0% -> 0%
where the time goes in v1:
time: 238 us
  waiting for transfers between devices  173 us (73%)
  matrix products  19.5 us (8%)
  between operations  14.1 us (6%)
  other arithmetic  13.5 us (6%)
  starting transfers between devices  11.4 us (5%)
  local copies, waits for them, and re-layouts  6.55 us (3%)
    ppermute x4, waiting for transfers between devices, partner(): lax.ppermute(value, axis, [(i, i ^ 1 << bit) for i in range(lax.axis_size...  165 us
    dot_general x1, matrix products, on_device(): jnp.dot(columns, lax.all_gather(coords, 'panel', axis=0, tiled=True).asty...  13.3 us
    all_to_all x1, waiting for transfers between devices, tiled_gather(): return lax.all_to_all(copies, axis, dim, dim, tiled=True)  7.5 us
    ppermute x4, starting transfers between devices, partner(): lax.ppermute(value, axis, [(i, i ^ 1 << bit) for i in range(lax.axis_size...  7.17 us
    add x1, other arithmetic, on_device(): merged = merged + partner(merged, 'leaf', level)  6.51 us
    dot_general x1, matrix products, on_device(): lax.dot_general(scaled, tiled_gather(coup, 'panel', 0), (((1,), (1,)), ((...  4.96 us
  transfers between devices with their start and end apart: 6, of which 4 were waited for; matrix products, arithmetic and copies ran while one was open for 6% of the time, Pallas kernels for 0%

profile of v1, /device:TPU:0, one launch (start us, length us, event | category | flops | bytes accessed | tf_op | source)
XLA Modules:
  0.0 237.8 jit_solution(8588037617949100608)
XLA Ops:
  6.5 2.1 pad_maximum_fusion
  8.6 4.2 %all-to-all-start = ((bf16[4,512,128]{2,1,0:T(8,128)(2,1)}), bf16[4,512,128]{2,1,0:T(8,128)(2,1)S(1)}, u32[]{:S(2)}, u32[]{:S(2)}) async-start(bf16[4,512,128]{2,1,0:T(8,128)(2,1)} %bitcast.6), calls=%async_computation | async-start | bytes 1048576 | tf_op jit(solution)/shard_map/all_to_all | solution.py:11
  13.5 0.7 fusion.9
  14.1 7.5 %all-to-all-done = bf16[4,512,128]{2,1,0:T(8,128)(2,1)S(1)} async-done(((bf16[4,512,128]{2,1,0:T(8,128)(2,1)}), bf16[4,512,128]{2,1,0:T(8,128)(2,1)S(1)}, u32[]{:S(2)}, u32[]{:S(2)}) %all-to-all-start) | async-done | bytes 524320 | tf_op jit(solution)/shard_map/all_to_all | solution.py:11
  21.6 5.0 %bitcast_subtract_fusion = f32[512,2048]{1,0:T(8,128)} fusion(f32[1,512,2048]{2,1,0:T(8,128)} %param.6, bf16[2048,128]{1,0:T(8,128)(2,1)S(1)} %bitcast.24, bf16[1,512,128]{2,1,0:T(8,128)(2,1)} %param.7, f32[128]{0:T(128)S(1)} %fusion.9), kind=kOutput, calls=%fused_computation.2 | convolution fusion | flops 269680640 | bytes 9044480 | tf_op jit(solution)/shard_map/dot_general | solution.py:41
  26.6 2.2 collective-permute-start.2
  28.8 0.0 copy-done
  28.8 1.2 fusion.3
  30.1 2.4 %constant_dynamic-slice_fusion.1 = f32[512,2048]{1,0:T(8,128)} fusion(f32[512,4096]{1,0:T(8,128)S(1)} %fusion.3, s32[]{:T(128)S(6)} %select_n.13), kind=kLoop, calls=%fused_computation.13 | loop fusion | bytes 8388612 | tf_op jit(solution)/shard_map/dynamic_slice | solution.py:25
  32.5 2.1 copy-done.1
  34.6 1.6 collective-permute-start
  36.1 0.0 all-gather.3.cloned.1.call-update
  36.2 83.2 %collective-permute-done.2 = f32[512,2048]{1,0:T(8,128)} collective-permute-done((f32[512,2048]{1,0:T(8,128)}, f32[512,2048]{1,0:T(8,128)}, u32[]{:S(2)}, u32[]{:S(2)}) %collective-permute-start.2) | collective-permute-done | bytes 4194336 | tf_op jit(solution)/shard_map/ppermute | solution.py:15
  119.4 6.5 %add.33 = f32[512,2048]{1,0:T(8,128)} add(f32[512,2048]{1,0:T(8,128)} %bitcast_subtract_fusion, f32[512,2048]{1,0:T(8,128)} %collective-permute-done.2) | non-fusion elementwise | flops 1048576 | bytes 12582912 | tf_op jit(solution)/shard_map/add | solution.py:49
  125.9 1.8 collective-permute-start.3
  127.7 0.0 collective-permute-done
  127.7 4.2 %dynamic-slice_add_fusion = f32[512,2048]{1,0:T(8,128)S(1)} fusion(f32[512,2048]{1,0:T(8,128)} %collective-permute-done, f32[512,4096]{1,0:T(8,128)} %copy-done.1, s32[]{:T(128)S(6)} %select_n.12), kind=kLoop, calls=%fused_computation.4 | loop fusion | flops 1048576 | bytes 12582916 | tf_op jit(solution)/shard_map/add | solution.py:26
  131.9 0.0 copy-start.2
  132.0 1.9 copy-done.2
  133.9 0.1 constant_dynamic-slice_fusion
  134.0 1.6 collective-permute-start.1
  135.6 44.5 %collective-permute-done.1 = f32[512,1024]{1,0:T(8,128)} collective-permute-done((f32[512,1024]{1,0:T(8,128)S(1)}, f32[512,1024]{1,0:T(8,128)}, u32[]{:S(2)}, u32[]{:S(2)}) %collective-permute-start.1) | collective-permute-done | bytes 2097184 | tf_op jit(solution)/shard_map/ppermute | solution.py:15
  180.1 37.6 %collective-permute-done.3 = f32[512,2048]{1,0:T(8,128)} collective-permute-done((f32[512,2048]{1,0:T(8,128)}, f32[512,2048]{1,0:T(8,128)}, u32[]{:S(2)}, u32[]{:S(2)}) %collective-permute-start.3) | collective-permute-done | bytes 4194336 | tf_op jit(solution)/shard_map/ppermute | solution.py:15
  217.7 13.3 %add_bitcast_fusion = f32[1,512,1024]{2,1,0:T(8,128)} fusion(f32[512,1024]{1,0:T(8,128)} %collective-permute-done.1, f32[512,2048]{1,0:T(8,128)} %copy-done.2, s32[]{:T(128)S(6)} %select_n.14, bf16[1,2048,1024]{2,1,0:T(8,128)(2,1)} %all-gather.3.cloned.1.call-done, f32[512,2048]{1,0:T(8,128)} %add.33, f32[512,2048]{1,0:T(8,128)} %collective-permute-done.3), kind=kOutput, calls=%fused_computation.5 | convolution fusion | flops 12886999040 | bytes 18874372 | tf_op jit(solution)/shard_map/dot_general | solution.py:52
  (6 shorter events, 0.0 us)
Async XLA Ops:
  6.5 22.3 %copy-start = (bf16[1,128,4096]{2,1,0:T(8,128)(2,1)S(1)}, bf16[1,128,4096]{2,1,0:T(8,128)(2,1)}, u32[]{:S(2)}) copy-start(bf16[1,128,4096]{2,1,0:T(8,128)(2,1)} %param.11) | copy-start | bytes 3145732
  8.6 13.1 %all-to-all-start = ((bf16[4,512,128]{2,1,0:T(8,128)(2,1)}), bf16[4,512,128]{2,1,0:T(8,128)(2,1)S(1)}, u32[]{:S(2)}, u32[]{:S(2)}) async-start(bf16[4,512,128]{2,1,0:T(8,128)(2,1)} %bitcast.6), calls=%async_computation | async-start | bytes 1048576 | tf_op jit(solution)/shard_map/all_to_all | solution.py:11
  12.8 167.3 %all-gather.3.cloned.1.call-start = ((), (), s32[]{:S(2)}) async-start(), calls=%async_computation.1 | async-start | bytes 5242880 | tf_op jit(solution)/shard_map/all_gather | solution.py:54
  21.6 7.2 %copy-start.3 = (bf16[1,512,128]{2,1,0:T(8,128)(2,1)S(1)}, bf16[1,512,128]{2,1,0:T(8,128)(2,1)}, u32[]{:S(2)}) copy-start(bf16[1,512,128]{2,1,0:T(8,128)(2,1)} %param.7) | copy-start | bytes 393220
  26.6 92.8 %collective-permute-start.2 = (f32[512,2048]{1,0:T(8,128)}, f32[512,2048]{1,0:T(8,128)}, u32[]{:S(2)}, u32[]{:S(2)}) collective-permute-start(f32[512,2048]{1,0:T(8,128)} %bitcast_subtract_fusion), channel_id=1, source_target_pairs={{0,4},{4,0},{8,12},{12,8},{16,20},{20,16},{24,28},{28,24},{1,5},{5... | collective-permute-start | bytes 12582920 | tf_op jit(solution)/shard_map/ppermute | solution.py:15
  30.1 4.5 %copy-start.1 = (f32[512,4096]{1,0:T(8,128)}, f32[512,4096]{1,0:T(8,128)S(1)}, u32[]{:S(2)}) copy-start(f32[512,4096]{1,0:T(8,128)S(1)} %fusion.3) | copy-start | bytes 25165828
  34.6 93.1 %collective-permute-start = (f32[512,2048]{1,0:T(8,128)}, f32[512,2048]{1,0:T(8,128)}, u32[]{:S(2)}, u32[]{:S(2)}) collective-permute-start(f32[512,2048]{1,0:T(8,128)} %constant_dynamic-slice_fusion.1), channel_id=1, source_target_pairs={{0,8},{4,12},{8,0},{12,4},{16,24},{20,28},{24,16},{28,20},{1,9},{5... | collective-permute-start | bytes 12582920 | tf_op jit(solution)/shard_map/ppermute | solution.py:15
  125.9 91.8 %collective-permute-start.3 = (f32[512,2048]{1,0:T(8,128)}, f32[512,2048]{1,0:T(8,128)}, u32[]{:S(2)}, u32[]{:S(2)}) collective-permute-start(f32[512,2048]{1,0:T(8,128)} %add.33), channel_id=1, source_target_pairs={{0,8},{4,12},{8,0},{12,4},{16,24},{20,28},{24,16},{28,20},{1,9},{5... | collective-permute-start | bytes 12582920 | tf_op jit(solution)/shard_map/ppermute | solution.py:15
  131.9 1.9 copy-start.2
  134.0 46.1 %collective-permute-start.1 = (f32[512,1024]{1,0:T(8,128)S(1)}, f32[512,1024]{1,0:T(8,128)}, u32[]{:S(2)}, u32[]{:S(2)}) collective-permute-start(f32[512,1024]{1,0:T(8,128)S(1)} %constant_dynamic-slice_fusion), channel_id=1, source_target_pairs={{0,4},{4,0},{8,12},{12,8},{16,20},{20,16},{24,28},{28,24},{1,5},{5... | collective-permute-start | bytes 6291464 | tf_op jit(solution)/shard_map/ppermute | solution.py:15
Sparse Core Ops, SparseCore 0:
  36.3 32.7 all-gather.2
